TPU v7x, 256 devices: a whole 4x4x8 slice. The times are simulated.
256 devices in a mesh: clip: 4 (over z_hi, core), fsdp: 64 (over y, z_lo, x).
Axes of the slice: x: 4, y: 4, z: 8 (z_hi: 2, z_lo: 4; z = z_hi * 4 + z_lo), core: 2. Of those that a mesh axis runs over, the one named last changes fastest.
Arguments:
- span_queries: bfloat16 [64, 512, 2560], P('fsdp', None, 'clip'), may hold values from -20 to 20
- span_keys: bfloat16 [64, 512, 2560], P('fsdp', None, 'clip'), may hold values from -12 to 12
- span_values: bfloat16 [64, 512, 2560], P('fsdp', None, 'clip'), may hold values from -6 to 6
- cache_keys: bfloat16 [128, 512, 2560], P(None, 'fsdp', 'clip'), may hold values from -6 to 6
- cache_values: bfloat16 [128, 512, 2560], P(None, 'fsdp', 'clip'), may hold values from -6 to 6
- page_table: int32 [128], replicated, may hold values from 0 to 127, each once
- frame_lists: int32 [64, 6], replicated, may hold values from 0 to 15, as said below
- list_counts: int32 [64], replicated, may hold values from 1 to 6, as said below
- out_weight: bfloat16 [2560, 5120], P('clip', 'fsdp'), may hold values from -1 to 1
Outputs:
- projected: bfloat16 [64, 512, 5120], P('fsdp', 'clip')
Inputs may be any that keep to these rules, and one draw needn't show every extreme that they name: `frame_lists`: each row holds 6 different cached frames; a frame attends to the first list_counts of them. `list_counts`: the counts of frames 2 * i and 2 * i + 1 sum to exactly 7; some frame attends to exactly 6. `page_table`: every block number once.
All inputs are finite; a program needn't handle non-finite values.
Results may differ from a plain program's by a relative error of at most 0.017.
Values may be sent and summed in bfloat16 or wider, within the bound.
No kernel may reach another device: no remote copies, remote signals or barrier semaphores. Data moves between devices by JAX's collectives and lax.ppermute only.
A program may use at most 128 MiB of HBM per device.

v0:
```python
import math
import jax
import jax.numpy as jnp
import numpy as np
from jax import lax
from jax.sharding import Mesh
from jax.sharding import PartitionSpec as P

HD = 128
CF = 8
NC = 16
FRAME_AXES = ("y", "zl", "x")
neg_fill = -1e30


def empty_state(tokens_here, heads_here):
    return (
        jnp.full((tokens_here, heads_here), neg_fill, jnp.float32),
        jnp.zeros((tokens_here, heads_here), jnp.float32),
        jnp.zeros((tokens_here, heads_here, HD), jnp.float32),
    )


def absorb(carried, query_block, key_block, value_block):
    running_max, running_sum, running_out = carried
    scores = jnp.einsum(
        "qhd,khd->qhk", query_block, key_block, preferred_element_type=jnp.float32
    ) * (1.0 / math.sqrt(HD))
    new_max = jnp.maximum(running_max, jnp.max(scores, axis=2))
    shrink = jnp.exp(running_max - new_max)
    weights = jnp.exp(scores - new_max[:, :, None])
    running_sum = running_sum * shrink + jnp.sum(weights, axis=2)
    running_out = running_out * shrink[:, :, None] + jnp.einsum(
        "qhk,khd->qhd",
        weights.astype(jnp.bfloat16),
        value_block,
        preferred_element_type=jnp.float32,
    )
    return (new_max, running_sum, running_out)


def pair_schedule(frames, half_slots, page_table, frame_lists, list_counts):
    dest = jnp.arange(frames, dtype=jnp.int32)[:, None]
    slot = jnp.arange(half_slots, dtype=jnp.int32)[None, :]
    even = dest - dest % 2
    global_half = dest % 2 * half_slots + slot
    combined = global_half // 2
    row_half = global_half % 2
    even_count = list_counts[even]
    for_even = combined < even_count
    listed_even = frame_lists[even, jnp.minimum(combined, frame_lists.shape[1] - 1)]
    listed_odd = frame_lists[even + 1, jnp.clip(combined - even_count, 0, frame_lists.shape[1] - 1)]
    listed = jnp.where(for_even, listed_even, listed_odd)
    blocks = page_table[even // CF * NC + listed]
    return (blocks, row_half, for_even)


def local(
    span_queries,
    span_keys,
    span_values,
    cache_keys,
    cache_values,
    page_table,
    frame_lists,
    list_counts,
    out_weight,
):
    frames = lax.axis_size(FRAME_AXES)
    own_frame = lax.axis_index(FRAME_AXES)
    tokens_here = span_queries.shape[1]
    row_width = span_queries.shape[2]
    heads_here = row_width // HD
    blocks_total, rows_here, _ = cache_keys.shape
    half_rows = rows_here // 2
    half_slots = frame_lists.shape[1] + 1
    own_queries = span_queries[0].reshape(tokens_here, heads_here, HD)
    own_keys = span_keys[0].reshape(tokens_here, heads_here, HD)
    own_values = span_values[0].reshape(tokens_here, heads_here, HD)
    blocks, row_half, for_even = pair_schedule(
        frames, half_slots, page_table, frame_lists, list_counts
    )
    split_keys = cache_keys.reshape(blocks_total, 2, half_rows, row_width)
    split_values = cache_values.reshape(blocks_total, 2, half_rows, row_width)
    sent = jnp.stack([split_keys[blocks, row_half], split_values[blocks, row_half]], axis=1)
    sent = sent.reshape(frames, -1, 128)
    arrived = lax.all_to_all(sent, FRAME_AXES, split_axis=0, concat_axis=0, tiled=True)
    arrived = arrived.reshape(frames, 2, half_slots, half_rows, heads_here, HD)
    arrived = arrived.transpose(1, 2, 0, 3, 4, 5).reshape(
        2, half_slots, frames * half_rows, heads_here, HD
    )
    arrived_keys = arrived[0]
    arrived_values = arrived[1]
    swap = [(i, i ^ 1) for i in range(lax.axis_size("x"))]
    partner_queries = lax.ppermute(own_queries, "x", swap)
    is_even = own_frame % 2 == 0
    mine = for_even[own_frame] == is_even
    own_state = absorb(empty_state(tokens_here, heads_here), own_queries, own_keys, own_values)
    other_state = empty_state(tokens_here, heads_here)

    def advance(slot, states):
        key_block = arrived_keys[slot]
        value_block = arrived_values[slot]

        def take_own(states):
            return (absorb(states[0], own_queries, key_block, value_block), states[1])

        def take_other(states):
            return (states[0], absorb(states[1], partner_queries, key_block, value_block))

        return lax.cond(mine[slot], take_own, take_other, states)

    own_state, other_state = lax.fori_loop(0, half_slots, advance, (own_state, other_state))
    got_max, got_sum, got_out = lax.ppermute(other_state, "x", swap)
    own_max, own_sum, own_out = own_state
    top = jnp.maximum(own_max, got_max)
    own_scale = jnp.exp(own_max - top)
    got_scale = jnp.exp(got_max - top)
    total_sum = own_sum * own_scale + got_sum * got_scale
    total_out = own_out * own_scale[:, :, None] + got_out * got_scale[:, :, None]
    attended = (
        (total_out / total_sum[:, :, None]).astype(jnp.bfloat16).reshape(tokens_here, row_width)
    )
    weight = out_weight
    for axis in reversed(FRAME_AXES):
        weight = lax.all_gather(weight, axis, axis=1, tiled=True)
    partial_value = jnp.dot(attended, weight, preferred_element_type=jnp.float32)
    own_rows = lax.psum_scatter(
        partial_value.astype(jnp.bfloat16), "clip", scatter_dimension=0, tiled=True
    )
    return own_rows[None]


def solution(mesh):
    frames = mesh.shape["fsdp"]
    fine = Mesh(
        np.asarray(mesh.devices).reshape(mesh.shape["clip"], frames // 16, 4, 4),
        ("clip",) + FRAME_AXES,
    )
    in_specs = (
        P(FRAME_AXES, None, "clip"),
        P(FRAME_AXES, None, "clip"),
        P(FRAME_AXES, None, "clip"),
        P(None, FRAME_AXES, "clip"),
        P(None, FRAME_AXES, "clip"),
        P(),
        P(),
        P(),
        P("clip", FRAME_AXES),
    )
    out_specs = P(FRAME_AXES, "clip", None)
    return jax.shard_map(local, mesh=fine, in_specs=in_specs, out_specs=out_specs, check_vma=False)
```

profile of v0, /device:TPU:1, one launch (start us, length us, event | category | flops | bytes accessed | tf_op | source)
XLA Modules:
  0.0 378.0 jit_solution(15196628837934634941)
XLA Ops:
  6.5 13.0 %all_gather.9 = bf16[640,320]{0,1:T(8,128)(2,1)} all-gather(bf16[640,80]{0,1:T(8,128)(2,1)} %param.21), channel_id=1, replica_groups=mesh['clip'=4,'y'=4,'zl'=4,'x'=4] {'x'}, dimensions={1}, use_global_device_ids=true | all-gather | bytes 512000 | tf_op jit(solution)/shard_map/all_gather | solution.py:126
  19.6 2.6 reshape.464
  23.3 2.3 gather_fusion.1
  25.9 2.3 gather_fusion.2
  28.8 3.0 gather_fusion.3
  32.2 2.6 reshape.463
  34.8 7.0 %gather_fusion.5 = bf16[448,4,640]{2,1,0:T(4,128)(2,1)} fusion(bf16[128,2,4,640]{3,2,1,0:T(4,128)(2,1)S(1)} %reshape.464, s32[448]{0:T(512)S(1)} %reshape.497), kind=kCustom, calls=%fused_computation.5 | custom fusion | bytes 4591104 | tf_op jit(solution)/shard_map/gather | solution.py:85
  41.8 7.1 %gather_fusion.4 = bf16[448,4,640]{2,1,0:T(4,128)(2,1)} fusion(bf16[128,2,4,640]{3,2,1,0:T(4,128)(2,1)S(1)} %reshape.463, s32[448]{0:T(512)S(1)} %reshape.497), kind=kCustom, calls=%fused_computation.4 | custom fusion | bytes 4591104 | tf_op jit(solution)/shard_map/gather | solution.py:85
  48.9 7.4 %pad_maximum_fusion = bf16[64,2,7,4,640]{4,3,2,1,0:T(4,128)(2,1)} fusion(bf16[64,1,7,4,640]{4,3,2,1,0:T(4,128)(2,1)} %bitcast.90, bf16[64,1,7,4,640]{4,3,2,1,0:T(4,128)(2,1)} %bitcast.91), kind=kLoop, calls=%fused_computation.39 | loop fusion | flops 2293760 | bytes 9175040 | tf_op jit(solution)/shard_map/stack | solution.py:85
  56.3 8.6 %reshape.465 = bf16[64,280,128]{2,1,0:T(8,128)(2,1)} reshape(bf16[64,2,7,4,640]{4,3,2,1,0:T(4,128)(2,1)} %pad_maximum_fusion) | data formatting | bytes 9175040 | tf_op jit(solution)/shard_map/reshape | solution.py:86
  65.0 10.6 %all-to-all-start = ((bf16[64,280,128]{2,1,0:T(8,128)(2,1)}), bf16[64,280,128]{2,1,0:T(8,128)(2,1)}, u32[]{:S(2)}, u32[]{:S(2)}) async-start(bf16[64,280,128]{2,1,0:T(8,128)(2,1)} %reshape.465), calls=%async_computation | async-start | bytes 9175040 | tf_op jit(solution)/shard_map/all_to_all | solution.py:87
  80.1 2.5 fusion.28
  82.6 1.4 copy.57
  84.0 2.1 copy.55
  87.6 40.7 %collective-permute-done = bf16[512,5,128]{0,2,1:T(8,128)(2,1)} collective-permute-done((bf16[512,5,128]{0,2,1:T(8,128)(2,1)S(1)}, bf16[512,5,128]{0,2,1:T(8,128)(2,1)}, u32[]{:S(2)}, u32[]{:S(2)}) %collective-permute-start) | collective-permute-done | bytes 655392 | tf_op jit(solution)/shard_map/ppermute | solution.py:95
  128.3 2.2 copy.56
  130.5 45.2 %all-to-all-done = bf16[64,280,128]{2,1,0:T(8,128)(2,1)} async-done(((bf16[64,280,128]{2,1,0:T(8,128)(2,1)}), bf16[64,280,128]{2,1,0:T(8,128)(2,1)}, u32[]{:S(2)}, u32[]{:S(2)}) %all-to-all-start) | async-done | bytes 4587552 | tf_op jit(solution)/shard_map/all_to_all | solution.py:87
  175.6 3.5 copy.52
  180.2 3.6 copy.53
  183.8 3.6 copy.54
  187.5 45.5 %while.23 = (s32[]{:T(128)}, f32[512,5]{0,1:T(8,128)S(1)}, f32[512,5]{0,1:T(8,128)S(1)}, f32[512,5,128]{2,1,0:T(8,128)S(1)}, f32[512,5]{0,1:T(8,128)S(1)}, /*ind...) while((s32[]{:T(128)}, f32[512,5]{0,1:T(8,128)S(1)}, ...), condition=%wide.region_9.10_spmd, body=%wide.region_2.9_spmd.sunk | while | flops 341447680 | bytes 15933780 | solution.py:113
  188.7 1.1 dynamic-slice_bitcast_fusion.3
  189.8 4.2 %conditional.2 = (f32[512,5]{0,1:T(8,128)S(1)}, f32[512,5]{0,1:T(8,128)S(1)}, f32[512,5,128]{2,1,0:T(8,128)S(1)}, f32[512,5]{0,1:T(8,128)S(1)}, f32[512,5]{0,1:T(8,128)S(1)}, /*index=5*/f32[512,5,128]{2,0,1:T(8,128)S(1)}) conditional(s32[]{:T(128)} %bitcast.88, (bf16[256,5,128]{2,0,1:T(8,128)(2,1)S(1)}, bf16[512,5,128]{2,0,1:T(8,128)(2,1)}, ...), branch_computations={%region_3.5_spmd, %region_6.8_spmd} | conditional | flops 341447680 | bytes 14602288 | solution.py:111
  189.9 1.8 bitcast_reduce_fusion.1
  195.3 1.1 dynamic-slice_bitcast_fusion.3
  196.5 4.2 %conditional.2 = (f32[512,5]{0,1:T(8,128)S(1)}, f32[512,5]{0,1:T(8,128)S(1)}, f32[512,5,128]{2,1,0:T(8,128)S(1)}, f32[512,5]{0,1:T(8,128)S(1)}, f32[512,5]{0,1:T(8,128)S(1)}, /*index=5*/f32[512,5,128]{2,0,1:T(8,128)S(1)}) conditional(s32[]{:T(128)} %bitcast.88, (bf16[256,5,128]{2,0,1:T(8,128)(2,1)S(1)}, bf16[512,5,128]{2,0,1:T(8,128)(2,1)}, ...), branch_computations={%region_3.5_spmd, %region_6.8_spmd} | conditional | flops 341447680 | bytes 14602288 | solution.py:111
  196.5 1.8 bitcast_reduce_fusion.1
  203.1 4.2 %conditional.2 = (f32[512,5]{0,1:T(8,128)S(1)}, f32[512,5]{0,1:T(8,128)S(1)}, f32[512,5,128]{2,1,0:T(8,128)S(1)}, f32[512,5]{0,1:T(8,128)S(1)}, f32[512,5]{0,1:T(8,128)S(1)}, /*index=5*/f32[512,5,128]{2,0,1:T(8,128)S(1)}) conditional(s32[]{:T(128)} %bitcast.88, (bf16[256,5,128]{2,0,1:T(8,128)(2,1)S(1)}, bf16[512,5,128]{2,0,1:T(8,128)(2,1)}, ...), branch_computations={%region_3.5_spmd, %region_6.8_spmd} | conditional | flops 341447680 | bytes 14602288 | solution.py:111
  203.1 1.7 bitcast_reduce_fusion.1
  208.6 1.1 dynamic-slice_bitcast_fusion.3
  209.7 4.2 %conditional.2 = (f32[512,5]{0,1:T(8,128)S(1)}, f32[512,5]{0,1:T(8,128)S(1)}, f32[512,5,128]{2,1,0:T(8,128)S(1)}, f32[512,5]{0,1:T(8,128)S(1)}, f32[512,5]{0,1:T(8,128)S(1)}, /*index=5*/f32[512,5,128]{2,0,1:T(8,128)S(1)}) conditional(s32[]{:T(128)} %bitcast.88, (bf16[256,5,128]{2,0,1:T(8,128)(2,1)S(1)}, bf16[512,5,128]{2,0,1:T(8,128)(2,1)}, ...), branch_computations={%region_3.5_spmd, %region_6.8_spmd} | conditional | flops 341447680 | bytes 14602288 | solution.py:111
  209.7 1.7 bitcast_reduce_fusion.1
  215.2 1.1 dynamic-slice_bitcast_fusion.3
  216.3 4.2 %conditional.2 = (f32[512,5]{0,1:T(8,128)S(1)}, f32[512,5]{0,1:T(8,128)S(1)}, f32[512,5,128]{2,1,0:T(8,128)S(1)}, f32[512,5]{0,1:T(8,128)S(1)}, f32[512,5]{0,1:T(8,128)S(1)}, /*index=5*/f32[512,5,128]{2,0,1:T(8,128)S(1)}) conditional(s32[]{:T(128)} %bitcast.88, (bf16[256,5,128]{2,0,1:T(8,128)(2,1)S(1)}, bf16[512,5,128]{2,0,1:T(8,128)(2,1)}, ...), branch_computations={%region_3.5_spmd, %region_6.8_spmd} | conditional | flops 341447680 | bytes 14602288 | solution.py:111
  216.3 1.8 bitcast_reduce_fusion.1
  221.8 1.1 dynamic-slice_bitcast_fusion.3
  222.9 4.2 %conditional.2 = (f32[512,5]{0,1:T(8,128)S(1)}, f32[512,5]{0,1:T(8,128)S(1)}, f32[512,5,128]{2,1,0:T(8,128)S(1)}, f32[512,5]{0,1:T(8,128)S(1)}, f32[512,5]{0,1:T(8,128)S(1)}, /*index=5*/f32[512,5,128]{2,0,1:T(8,128)S(1)}) conditional(s32[]{:T(128)} %bitcast.88, (bf16[256,5,128]{2,0,1:T(8,128)(2,1)S(1)}, bf16[512,5,128]{2,0,1:T(8,128)(2,1)}, ...), branch_computations={%region_3.5_spmd, %region_6.8_spmd} | conditional | flops 341447680 | bytes 14602288 | solution.py:111
  223.0 1.8 bitcast_reduce_fusion.1
  228.4 1.1 dynamic-slice_bitcast_fusion.3
  229.5 3.2 conditional.2
  229.6 1.6 bitcast_reduce_fusion
  233.0 1.5 copy.59
  234.5 2.2 collective-permute-start.2
  236.7 1.4 collective-permute-start.1
  238.8 23.3 %collective-permute-done.3 = f32[512,5]{0,1:T(8,128)S(1)} collective-permute-done((f32[512,5]{0,1:T(8,128)S(1)}, f32[512,5]{0,1:T(8,128)S(1)}, u32[]{:S(2)}, u32[]{:S(2)}) %collective-permute-start.3) | collective-permute-done | bytes 10272 | tf_op jit(solution)/shard_map/ppermute | solution.py:114
  262.5 1.7 divide_convert_fusion
  264.2 8.9 %convolution_convert_fusion = bf16[512,5120]{1,0:T(8,128)(2,1)} fusion(bf16[512,640]{0,1:T(8,128)(2,1)S(1)} %bitcast.99, bf16[640,5120]{0,1:T(8,128)(2,1)} %all-gather.5.cloned.1.call-done), kind=kOutput, calls=%fused_computation.35 | convolution fusion | flops 3358064640 | bytes 12451840 | tf_op jit(solution)/shard_map/dot_general | solution.py:127
  273.2 98.3 %reduce-scatter.2.cloned.1.call-done = bf16[128,5120]{1,0:T(8,128)(2,1)} async-done(((bf16[512,5120]{1,0:T(8,128)(2,1)}), bf16[128,5120]{1,0:T(8,128)(2,1)}) %reduce-scatter.2.cloned.1.call-update) | async-done | bytes 1310736 | tf_op jit(solution)/shard_map/reduce_scatter | solution.py:128
  (120 shorter events, 31.7 us)
Async XLA Ops:
  6.5 16.8 %copy-start = (s32[64,6]{0,1:T(8,128)S(1)}, s32[64,6]{0,1:T(8,128)}, u32[]{:S(2)}) copy-start(s32[64,6]{0,1:T(8,128)} %param.19) | copy-start | bytes 4612
  6.5 15.7 %copy-start.3 = (s32[64]{0:T(128)S(1)}, s32[64]{0:T(128)}, u32[]{:S(2)}) copy-start(s32[64]{0:T(128)} %param.20) | copy-start | bytes 772
  6.5 69.1 %all-gather.3.cloned.1.call-start = ((), (), s32[]{:S(2)}) async-start(), calls=%async_computation.2 | async-start | bytes 2048000 | tf_op jit(solution)/shard_map/all_gather | solution.py:126
  28.2 0.7 copy-start.2
  65.0 11.4 %copy-start.4 = (bf16[1,512,640]{2,1,0:T(8,128)(2,1)S(1)}, bf16[1,512,640]{2,1,0:T(8,128)(2,1)}, u32[]{:S(2)}) copy-start(bf16[1,512,640]{2,1,0:T(8,128)(2,1)} %param.13) | copy-start | bytes 1966084
  65.0 110.6 %all-to-all-start = ((bf16[64,280,128]{2,1,0:T(8,128)(2,1)}), bf16[64,280,128]{2,1,0:T(8,128)(2,1)}, u32[]{:S(2)}, u32[]{:S(2)}) async-start(bf16[64,280,128]{2,1,0:T(8,128)(2,1)} %reshape.465), calls=%async_computation | async-start | bytes 9175040 | tf_op jit(solution)/shard_map/all_to_all | solution.py:87
  75.6 2.1 copy-start.5
  75.6 2.4 copy-start.6
  75.6 188.6 %all-gather.5.cloned.1.call-start = ((), (), s32[]{:S(2)}) async-start(), calls=%async_computation.3 | async-start | bytes 8192000 | tf_op jit(solution)/shard_map/all_gather | solution.py:126
  76.4 295.1 %reduce-scatter.2.cloned.1.call-start = ((), (), s32[]{:S(2)}) async-start(), calls=%async_computation.4 | async-start | bytes 6553600 | tf_op jit(solution)/shard_map/reduce_scatter | solution.py:128
  76.7 51.6 %collective-permute-start = (bf16[512,5,128]{0,2,1:T(8,128)(2,1)S(1)}, bf16[512,5,128]{0,2,1:T(8,128)(2,1)}, u32[]{:S(2)}, u32[]{:S(2)}) collective-permute-start(bf16[512,5,128]{0,2,1:T(8,128)(2,1)S(1)} %bitcast.94), channel_id=1, source_target_pairs={{0,1},{1,0},{2,3},{3,2},{4,5},{5,4},{6,7},{7,6},{8,9},{9,8},{10,11... | collective-permute-start | bytes 1966088 | tf_op jit(solution)/shard_map/ppermute | solution.py:95
  234.5 28.0 %collective-permute-start.2 = (f32[512,5,128]{0,2,1:T(8,128)}, f32[512,5,128]{0,2,1:T(8,128)}, u32[]{:S(2)}, u32[]{:S(2)}) collective-permute-start(f32[512,5,128]{0,2,1:T(8,128)} %copy.59), channel_id=1, source_target_pairs={{0,1},{1,0},{2,3},{3,2},{4,5},{5,4},{6,7},{7,6},{8,9},{9,8},{10,11... | collective-permute-start | bytes 3932168 | tf_op jit(solution)/shard_map/ppermute | solution.py:114
  236.7 25.4 %collective-permute-start.3 = (f32[512,5]{0,1:T(8,128)S(1)}, f32[512,5]{0,1:T(8,128)S(1)}, u32[]{:S(2)}, u32[]{:S(2)}) collective-permute-start(f32[512,5]{0,1:T(8,128)S(1)} %get-tuple-element.286), channel_id=1, source_target_pairs={{0,1},{1,0},{2,3},{3,2},{4,5},{5,4},{6,7},{7,6},{8,9},{9,8},{10,11... | collective-permute-start | bytes 30728 | tf_op jit(solution)/shard_map/ppermute | solution.py:114
  236.7 25.7 %collective-permute-start.1 = (f32[512,5]{0,1:T(8,128)S(1)}, f32[512,5]{0,1:T(8,128)S(1)}, u32[]{:S(2)}, u32[]{:S(2)}) collective-permute-start(f32[512,5]{0,1:T(8,128)S(1)} %get-tuple-element.283), channel_id=1, source_target_pairs={{0,1},{1,0},{2,3},{3,2},{4,5},{5,4},{6,7},{7,6},{8,9},{9,8},{10,11... | collective-permute-start | bytes 30728 | tf_op jit(solution)/shard_map/ppermute | solution.py:114
  273.1 98.3 %copy-start.1 = (s32[64,6]{0,1:T(8,128)S(1)}, s32[64,6]{0,1:T(8,128)}, u32[]{:S(2)}) copy-start(s32[64,6]{0,1:T(8,128)} %param.19) | copy-start | bytes 4612
Sparse Core Ops, SparseCore 0:
  19.7 46.3 all-gather.2
  78.2 106.0 all-gather.4
  273.3 98.1 reduce-scatter.1
where the time goes:
time: 379 us; the launch traced here: 378 us
  waiting for transfers between devices  209 us (55%)
  local copies, waits for them, and re-layouts  75.5 us (20%)
  matrix products  32.2 us (8%)
  starting transfers between devices  15.4 us (4%)
  other arithmetic  14.5 us (4%)
  between operations  13.4 us (4%)
  blocking collectives  13 us (3%)
  loops' own time  5.42 us (1%)
    reduce_scatter x1, waiting for transfers between devices, local(): lax.psum_scatter(partial_value.astype(jnp.bfloat16), 'clip', scatter_dime...  98.3 us
    all_to_all x1, waiting for transfers between devices, local(): lax.all_to_all(sent, FRAME_AXES, split_axis=0, concat_axis=0, tiled=True)  45.2 us
    ppermute x1, waiting for transfers between devices, local(): partner_queries = lax.ppermute(own_queries, 'x', swap)  40.7 us
    ppermute x3, waiting for transfers between devices, local(): got_max, got_sum, got_out = lax.ppermute(other_state, 'x', swap)  23.6 us
    dot_general x8, matrix products, absorb(): jnp.einsum('qhd,khd->qhk', query_block, key_block, preferred_element_type...  13 us
    all_gather x1, blocking collectives, local(): weight = lax.all_gather(weight, axis, axis=1, tiled=True)  13 us
    all_to_all x1, starting transfers between devices, local(): lax.all_to_all(sent, FRAME_AXES, split_axis=0, concat_axis=0, tiled=True)  10.6 us
    dot_general x8, matrix products, absorb(): jnp.einsum('qhk,khd->qhd', weights.astype(jnp.bfloat16), value_block, pre...  10.3 us
  transfers between devices with their start and end apart: 8, of which 5 were waited for; matrix products, arithmetic and copies ran while one was open for 30% of the time, Pallas kernels for 0%

commit v1 on v0

--- a/solution.py
+++ b/solution.py
@@ -123,7 +123,16 @@
     )
     weight = out_weight
     for axis in reversed(FRAME_AXES):
-        weight = lax.all_gather(weight, axis, axis=1, tiled=True)
+        view_page = lambda incoming_x, lane_axis, axis_no: jnp.concatenate(
+            jax.lax.all_to_all(
+                jnp.stack([incoming_x for _ in range(jax.lax.axis_size(lane_axis))]),
+                axis_name=lane_axis,
+                split_axis=0,
+                concat_axis=0,
+            ),
+            axis=axis_no,
+        )
+        weight = view_page(weight, axis, 1)
     partial_value = jnp.dot(attended, weight, preferred_element_type=jnp.float32)
     own_rows = lax.psum_scatter(
         partial_value.astype(jnp.bfloat16), "clip", scatter_dimension=0, tiled=True

time: 379 us -> 414 us (1.092)
  waiting for transfers between devices: 209 us -> 225 us
  starting transfers between devices: 15.4 us -> 24.4 us
  local copies, waits for them, and re-layouts: 75.5 us -> 80.8 us
    all_to_all x1, waiting for transfers between devices: 45.2 us -> 99.8 us  [local(): lax.all_to_all(sent, FRAME_AXES, split_axis=0, concat_axis=0, tiled=True)]
    ppermute x1, waiting for transfers between devices: 40.7 us -> 0.01 us  [local(): partner_queries = lax.ppermute(own_queries, 'x', swap)]
    all_gather x1 -> x0, blocking collectives: 13 us -> none  [local(): weight = lax.all_gather(weight, axis, axis=1, tiled=True)]
    all_to_all x0 -> x1, blocking collectives: none -> 11.9 us  [local(): jax.lax.all_to_all(jnp.stack([incoming_x for _ in range(jax.lax.axis_size...]
    all_to_all x0 -> x2, starting transfers between devices: none -> 11 us  [local(): jax.lax.all_to_all(jnp.stack([incoming_x for _ in range(jax.lax.axis_size...]
    another operation x9 -> x12, local copies, waits for them, and re-layouts: 4.97 us -> 11.9 us  [the longest x3 6.96 us: local(): jnp.stack([incoming_x for _ in range(jax.lax.axis_size(lane_axis))])]
  transfers between devices with their start and end apart: 8 -> 8, of which waited for: 5 -> 4; matrix products, arithmetic and copies ran while one was open for 30% -> 29% of each run, Pallas kernels for 0% -> 0%
where the time goes in v1:
time: 414 us; the launch traced here: 413 us
  waiting for transfers between devices  225 us (54%)
  local copies, waits for them, and re-layouts  80.8 us (20%)
  matrix products  34.5 us (8%)
  starting transfers between devices  24.4 us (6%)
  other arithmetic  17.1 us (4%)
  between operations  13.7 us (3%)
  blocking collectives  11.9 us (3%)
  loops' own time  5.83 us (1%)
    reduce_scatter x1, waiting for transfers between devices, local(): lax.psum_scatter(partial_value.astype(jnp.bfloat16), 'clip', scatter_dime...  101 us
    all_to_all x1, waiting for transfers between devices, local(): lax.all_to_all(sent, FRAME_AXES, split_axis=0, concat_axis=0, tiled=True)  99.8 us
    ppermute x3, waiting for transfers between devices, local(): got_max, got_sum, got_out = lax.ppermute(other_state, 'x', swap)  23.8 us
    dot_general x8, matrix products, absorb(): jnp.einsum('qhd,khd->qhk', query_block, key_block, preferred_element_type...  15.3 us
    all_to_all x1, blocking collectives, local(): jax.lax.all_to_all(jnp.stack([incoming_x for _ in range(jax.lax.axis_size...  11.9 us
    all_to_all x2, starting transfers between devices, local(): jax.lax.all_to_all(jnp.stack([incoming_x for _ in range(jax.lax.axis_size...  11 us
    dot_general x8, matrix products, absorb(): jnp.einsum('qhk,khd->qhd', weights.astype(jnp.bfloat16), value_block, pre...  10.3 us
    all_to_all x1, starting transfers between devices, local(): lax.all_to_all(sent, FRAME_AXES, split_axis=0, concat_axis=0, tiled=True)  9.41 us
  transfers between devices with their start and end apart: 8, of which 4 were waited for; matrix products, arithmetic and copies ran while one was open for 29% of the time, Pallas kernels for 0%

profile of v1, /device:TPU:1, one launch (start us, length us, event | category | flops | bytes accessed | tf_op | source)
XLA Modules:
  0.0 412.9 jit_solution(1879173500305536432)
XLA Ops:
  7.5 11.9 %all_to_all.20 = bf16[4,640,80]{1,2,0:T(8,128)(2,1)S(1)} all-to-all(bf16[4,640,80]{1,2,0:T(8,128)(2,1)S(1)} %stack.25), channel_id=1, replica_groups=mesh['clip'=4,'y'=4,'zl'=4,'x'=4] {'x'}, dimensions={0} | all-to-all | bytes 819200 | tf_op jit(solution)/shard_map/all_to_all | solution.py:127
  19.3 1.3 stack.26
  20.7 5.7 %all-to-all-start.2 = ((bf16[4,640,320]{1,2,0:T(8,128)(2,1)}), bf16[4,640,320]{1,2,0:T(8,128)(2,1)}, u32[]{:S(2)}, u32[]{:S(2)}) async-start(bf16[4,640,320]{1,2,0:T(8,128)(2,1)} %stack.26), calls=%async_computation.2 | async-start | bytes 3276800 | tf_op jit(solution)/shard_map/all_to_all | solution.py:127
  27.9 2.3 gather_fusion.1
  30.4 2.3 gather_fusion.2
  33.4 3.0 gather_fusion.3
  36.8 2.6 reshape.481
  39.4 7.0 %gather_fusion.5 = bf16[448,4,640]{2,1,0:T(4,128)(2,1)} fusion(bf16[128,2,4,640]{3,2,1,0:T(4,128)(2,1)S(1)} %reshape.482, s32[448]{0:T(512)S(1)} %reshape.519), kind=kCustom, calls=%fused_computation.5 | custom fusion | bytes 4591104 | tf_op jit(solution)/shard_map/gather | solution.py:85
  46.4 7.0 %gather_fusion.4 = bf16[448,4,640]{2,1,0:T(4,128)(2,1)} fusion(bf16[128,2,4,640]{3,2,1,0:T(4,128)(2,1)S(1)} %reshape.481, s32[448]{0:T(512)S(1)} %reshape.519), kind=kCustom, calls=%fused_computation.4 | custom fusion | bytes 4591104 | tf_op jit(solution)/shard_map/gather | solution.py:85
  53.3 7.4 %pad_maximum_fusion = bf16[64,2,7,4,640]{4,3,2,1,0:T(4,128)(2,1)} fusion(bf16[64,1,7,4,640]{4,3,2,1,0:T(4,128)(2,1)} %bitcast.99, bf16[64,1,7,4,640]{4,3,2,1,0:T(4,128)(2,1)} %bitcast.100), kind=kLoop, calls=%fused_computation.39 | loop fusion | flops 2293760 | bytes 9175040 | tf_op jit(solution)/shard_map/stack | solution.py:85
  60.8 8.6 %reshape.483 = bf16[64,280,128]{2,1,0:T(8,128)(2,1)} reshape(bf16[64,2,7,4,640]{4,3,2,1,0:T(4,128)(2,1)} %pad_maximum_fusion) | data formatting | bytes 9175040 | tf_op jit(solution)/shard_map/reshape | solution.py:86
  69.4 9.4 %all-to-all-start = ((bf16[64,280,128]{2,1,0:T(8,128)(2,1)}), bf16[64,280,128]{2,1,0:T(8,128)(2,1)}, u32[]{:S(2)}, u32[]{:S(2)}) async-start(bf16[64,280,128]{2,1,0:T(8,128)(2,1)} %reshape.483), calls=%async_computation | async-start | bytes 9175040 | tf_op jit(solution)/shard_map/all_to_all | solution.py:87
  80.4 99.8 %all-to-all-done = bf16[64,280,128]{2,1,0:T(8,128)(2,1)} async-done(((bf16[64,280,128]{2,1,0:T(8,128)(2,1)}), bf16[64,280,128]{2,1,0:T(8,128)(2,1)}, u32[]{:S(2)}, u32[]{:S(2)}) %all-to-all-start) | async-done | bytes 4587552 | tf_op jit(solution)/shard_map/all_to_all | solution.py:87
  180.3 4.7 %stack.27 = bf16[4,640,1280]{1,2,0:T(8,128)(2,1)} broadcast(bf16[640,1280]{0,1:T(8,128)(2,1)} %bitcast.25), dimensions={1,2} | broadcast | bytes 8192000 | tf_op jit(solution)/shard_map/stack | solution.py:128
  185.0 5.3 %all-to-all-start.3 = ((bf16[4,640,1280]{1,2,0:T(8,128)(2,1)}), bf16[4,640,1280]{1,2,0:T(8,128)(2,1)}, u32[]{:S(2)}, u32[]{:S(2)}) async-start(bf16[4,640,1280]{1,2,0:T(8,128)(2,1)} %stack.27), calls=%async_computation.3 | async-start | bytes 13107200 | tf_op jit(solution)/shard_map/all_to_all | solution.py:127
  190.3 3.2 bitcast_reduce_fusion.2
  193.8 3.5 fusion.20
  197.8 2.5 fusion.28
  200.3 1.4 copy.58
  201.8 2.1 copy.56
  205.3 2.2 copy.57
  207.5 3.5 copy.53
  212.1 3.5 copy.54
  215.6 3.5 copy.55
  219.2 46.4 %while.23 = (s32[]{:T(128)}, f32[512,5]{0,1:T(8,128)S(1)}, f32[512,5]{0,1:T(8,128)S(1)}, f32[512,5,128]{2,1,0:T(8,128)S(1)}, f32[512,5]{0,1:T(8,128)S(1)}, /*ind...) while((s32[]{:T(128)}, f32[512,5]{0,1:T(8,128)S(1)}, ...), condition=%wide.region_9.10_spmd, body=%wide.region_2.9_spmd.sunk | while | flops 341447680 | bytes 15933780 | solution.py:113
  221.7 4.2 %conditional.2 = (f32[512,5]{0,1:T(8,128)S(1)}, f32[512,5]{0,1:T(8,128)S(1)}, f32[512,5,128]{2,1,0:T(8,128)S(1)}, f32[512,5]{0,1:T(8,128)S(1)}, f32[512,5]{0,1:T(8,128)S(1)}, /*index=5*/f32[512,5,128]{2,0,1:T(8,128)S(1)}) conditional(s32[]{:T(128)} %bitcast.97, (bf16[256,5,128]{2,0,1:T(8,128)(2,1)S(1)}, bf16[512,5,128]{2,0,1:T(8,128)(2,1)}, ...), branch_computations={%region_3.5_spmd, %region_6.8_spmd} | conditional | flops 341447680 | bytes 14602288 | solution.py:111
  221.7 1.7 bitcast_reduce_fusion.1
  227.3 1.1 dynamic-slice_bitcast_fusion.3
  228.5 4.2 %conditional.2 = (f32[512,5]{0,1:T(8,128)S(1)}, f32[512,5]{0,1:T(8,128)S(1)}, f32[512,5,128]{2,1,0:T(8,128)S(1)}, f32[512,5]{0,1:T(8,128)S(1)}, f32[512,5]{0,1:T(8,128)S(1)}, /*index=5*/f32[512,5,128]{2,0,1:T(8,128)S(1)}) conditional(s32[]{:T(128)} %bitcast.97, (bf16[256,5,128]{2,0,1:T(8,128)(2,1)S(1)}, bf16[512,5,128]{2,0,1:T(8,128)(2,1)}, ...), branch_computations={%region_3.5_spmd, %region_6.8_spmd} | conditional | flops 341447680 | bytes 14602288 | solution.py:111
  228.5 1.8 bitcast_reduce_fusion.1
  234.1 1.1 dynamic-slice_bitcast_fusion.3
  235.2 4.2 %conditional.2 = (f32[512,5]{0,1:T(8,128)S(1)}, f32[512,5]{0,1:T(8,128)S(1)}, f32[512,5,128]{2,1,0:T(8,128)S(1)}, f32[512,5]{0,1:T(8,128)S(1)}, f32[512,5]{0,1:T(8,128)S(1)}, /*index=5*/f32[512,5,128]{2,0,1:T(8,128)S(1)}) conditional(s32[]{:T(128)} %bitcast.97, (bf16[256,5,128]{2,0,1:T(8,128)(2,1)S(1)}, bf16[512,5,128]{2,0,1:T(8,128)(2,1)}, ...), branch_computations={%region_3.5_spmd, %region_6.8_spmd} | conditional | flops 341447680 | bytes 14602288 | solution.py:111
  235.2 1.7 bitcast_reduce_fusion.1
  241.9 4.2 %conditional.2 = (f32[512,5]{0,1:T(8,128)S(1)}, f32[512,5]{0,1:T(8,128)S(1)}, f32[512,5,128]{2,1,0:T(8,128)S(1)}, f32[512,5]{0,1:T(8,128)S(1)}, f32[512,5]{0,1:T(8,128)S(1)}, /*index=5*/f32[512,5,128]{2,0,1:T(8,128)S(1)}) conditional(s32[]{:T(128)} %bitcast.97, (bf16[256,5,128]{2,0,1:T(8,128)(2,1)S(1)}, bf16[512,5,128]{2,0,1:T(8,128)(2,1)}, ...), branch_computations={%region_3.5_spmd, %region_6.8_spmd} | conditional | flops 341447680 | bytes 14602288 | solution.py:111
  242.0 1.8 bitcast_reduce_fusion.1
  248.7 4.2 %conditional.2 = (f32[512,5]{0,1:T(8,128)S(1)}, f32[512,5]{0,1:T(8,128)S(1)}, f32[512,5,128]{2,1,0:T(8,128)S(1)}, f32[512,5]{0,1:T(8,128)S(1)}, f32[512,5]{0,1:T(8,128)S(1)}, /*index=5*/f32[512,5,128]{2,0,1:T(8,128)S(1)}) conditional(s32[]{:T(128)} %bitcast.97, (bf16[256,5,128]{2,0,1:T(8,128)(2,1)S(1)}, bf16[512,5,128]{2,0,1:T(8,128)(2,1)}, ...), branch_computations={%region_3.5_spmd, %region_6.8_spmd} | conditional | flops 341447680 | bytes 14602288 | solution.py:111
  248.7 1.8 bitcast_reduce_fusion.1
  255.4 4.2 %conditional.2 = (f32[512,5]{0,1:T(8,128)S(1)}, f32[512,5]{0,1:T(8,128)S(1)}, f32[512,5,128]{2,1,0:T(8,128)S(1)}, f32[512,5]{0,1:T(8,128)S(1)}, f32[512,5]{0,1:T(8,128)S(1)}, /*index=5*/f32[512,5,128]{2,0,1:T(8,128)S(1)}) conditional(s32[]{:T(128)} %bitcast.97, (bf16[256,5,128]{2,0,1:T(8,128)(2,1)S(1)}, bf16[512,5,128]{2,0,1:T(8,128)(2,1)}, ...), branch_computations={%region_3.5_spmd, %region_6.8_spmd} | conditional | flops 341447680 | bytes 14602288 | solution.py:111
  255.4 1.8 bitcast_reduce_fusion.1
  262.2 3.2 conditional.2
  262.2 1.6 bitcast_reduce_fusion
  265.6 1.5 copy.60
  267.1 1.4 collective-permute-start.2
  268.5 1.4 collective-permute-start.1
  270.6 23.5 %collective-permute-done.3 = f32[512,5]{0,1:T(8,128)S(1)} collective-permute-done((f32[512,5]{0,1:T(8,128)S(1)}, f32[512,5]{0,1:T(8,128)S(1)}, u32[]{:S(2)}, u32[]{:S(2)}) %collective-permute-start.3) | collective-permute-done | bytes 10272 | tf_op jit(solution)/shard_map/ppermute | solution.py:114
  294.4 1.7 divide_convert_fusion
  296.1 9.0 %convolution_convert_fusion = bf16[512,5120]{1,0:T(8,128)(2,1)} fusion(bf16[512,640]{0,1:T(8,128)(2,1)S(1)} %bitcast.109, bf16[640,5120]{0,1:T(8,128)(2,1)} %bitcast.27), kind=kOutput, calls=%fused_computation.35 | convolution fusion | flops 3358064640 | bytes 12451840 | tf_op jit(solution)/shard_map/dot_general | solution.py:136
  305.1 100.9 %reduce-scatter.2.cloned.1.call-done = bf16[128,5120]{1,0:T(8,128)(2,1)} async-done(((bf16[512,5120]{1,0:T(8,128)(2,1)}), bf16[128,5120]{1,0:T(8,128)(2,1)}) %reduce-scatter.2.cloned.1.call-update) | async-done | bytes 1310736 | tf_op jit(solution)/shard_map/reduce_scatter | solution.py:137
  (125 shorter events, 35.9 us)
Async XLA Ops:
  6.5 21.3 %copy-start = (s32[64,6]{0,1:T(8,128)S(1)}, s32[64,6]{0,1:T(8,128)}, u32[]{:S(2)}) copy-start(s32[64,6]{0,1:T(8,128)} %param.19) | copy-start | bytes 4612
  19.3 7.1 %copy-start.5 = (bf16[128,8,640]{2,1,0:T(8,128)(2,1)S(1)}, bf16[128,8,640]{2,1,0:T(8,128)(2,1)}, u32[]{:S(2)}) copy-start(bf16[128,8,640]{2,1,0:T(8,128)(2,1)} %param.17) | copy-start | bytes 3932164
  20.7 6.1 %copy-start.3 = (s32[64]{0:T(128)S(1)}, s32[64]{0:T(128)}, u32[]{:S(2)}) copy-start(s32[64]{0:T(128)} %param.20) | copy-start | bytes 772
  20.7 48.8 %all-to-all-start.2 = ((bf16[4,640,320]{1,2,0:T(8,128)(2,1)}), bf16[4,640,320]{1,2,0:T(8,128)(2,1)}, u32[]{:S(2)}, u32[]{:S(2)}) async-start(bf16[4,640,320]{1,2,0:T(8,128)(2,1)} %stack.26), calls=%async_computation.2 | async-start | bytes 3276800 | tf_op jit(solution)/shard_map/all_to_all | solution.py:127
  32.7 0.7 copy-start.2
  69.4 9.4 %copy-start.6 = (bf16[1,512,640]{2,1,0:T(8,128)(2,1)S(1)}, bf16[1,512,640]{2,1,0:T(8,128)(2,1)}, u32[]{:S(2)}) copy-start(bf16[1,512,640]{2,1,0:T(8,128)(2,1)} %param.13) | copy-start | bytes 1966084
  69.4 10.7 %copy-start.7 = (bf16[1,512,640]{2,1,0:T(8,128)(2,1)S(1)}, bf16[1,512,640]{2,1,0:T(8,128)(2,1)}, u32[]{:S(2)}) copy-start(bf16[1,512,640]{2,1,0:T(8,128)(2,1)} %param.14) | copy-start | bytes 1966084
  69.4 110.8 %all-to-all-start = ((bf16[64,280,128]{2,1,0:T(8,128)(2,1)}), bf16[64,280,128]{2,1,0:T(8,128)(2,1)}, u32[]{:S(2)}, u32[]{:S(2)}) async-start(bf16[64,280,128]{2,1,0:T(8,128)(2,1)} %reshape.483), calls=%async_computation | async-start | bytes 9175040 | tf_op jit(solution)/shard_map/all_to_all | solution.py:87
  79.1 126.2 %collective-permute-start = (bf16[512,5,128]{0,2,1:T(8,128)(2,1)S(1)}, bf16[512,5,128]{0,2,1:T(8,128)(2,1)}, u32[]{:S(2)}, u32[]{:S(2)}) collective-permute-start(bf16[512,5,128]{0,2,1:T(8,128)(2,1)S(1)} %bitcast.103), channel_id=1, source_target_pairs={{0,1},{1,0},{2,3},{3,2},{4,5},{5,4},{6,7},{7,6},{8,9},{9,8},{10,11... | collective-permute-start | bytes 1966088 | tf_op jit(solution)/shard_map/ppermute | solution.py:95
  185.0 111.2 %all-to-all-start.3 = ((bf16[4,640,1280]{1,2,0:T(8,128)(2,1)}), bf16[4,640,1280]{1,2,0:T(8,128)(2,1)}, u32[]{:S(2)}, u32[]{:S(2)}) async-start(bf16[4,640,1280]{1,2,0:T(8,128)(2,1)} %stack.27), calls=%async_computation.3 | async-start | bytes 13107200 | tf_op jit(solution)/shard_map/all_to_all | solution.py:127
  190.3 215.8 %reduce-scatter.2.cloned.1.call-start = ((), (), s32[]{:S(2)}) async-start(), calls=%async_computation.5 | async-start | bytes 6553600 | tf_op jit(solution)/shard_map/reduce_scatter | solution.py:137
  190.3 3.2 copy-start.8
  193.8 4.0 copy-start.4
  267.1 27.3 %collective-permute-start.2 = (f32[512,5,128]{0,2,1:T(8,128)}, f32[512,5,128]{0,2,1:T(8,128)}, u32[]{:S(2)}, u32[]{:S(2)}) collective-permute-start(f32[512,5,128]{0,2,1:T(8,128)} %copy.60), channel_id=1, source_target_pairs={{0,1},{1,0},{2,3},{3,2},{4,5},{5,4},{6,7},{7,6},{8,9},{9,8},{10,11... | collective-permute-start | bytes 3932168 | tf_op jit(solution)/shard_map/ppermute | solution.py:114
  268.4 25.6 %collective-permute-start.3 = (f32[512,5]{0,1:T(8,128)S(1)}, f32[512,5]{0,1:T(8,128)S(1)}, u32[]{:S(2)}, u32[]{:S(2)}) collective-permute-start(f32[512,5]{0,1:T(8,128)S(1)} %get-tuple-element.286), channel_id=1, source_target_pairs={{0,1},{1,0},{2,3},{3,2},{4,5},{5,4},{6,7},{7,6},{8,9},{9,8},{10,11... | collective-permute-start | bytes 30728 | tf_op jit(solution)/shard_map/ppermute | solution.py:114
  268.5 25.9 %collective-permute-start.1 = (f32[512,5]{0,1:T(8,128)S(1)}, f32[512,5]{0,1:T(8,128)S(1)}, u32[]{:S(2)}, u32[]{:S(2)}) collective-permute-start(f32[512,5]{0,1:T(8,128)S(1)} %get-tuple-element.283), channel_id=1, source_target_pairs={{0,1},{1,0},{2,3},{3,2},{4,5},{5,4},{6,7},{7,6},{8,9},{9,8},{10,11... | collective-permute-start | bytes 30728 | tf_op jit(solution)/shard_map/ppermute | solution.py:114
  305.1 101.0 %copy-start.1 = (s32[64,6]{0,1:T(8,128)S(1)}, s32[64,6]{0,1:T(8,128)}, u32[]{:S(2)}) copy-start(s32[64,6]{0,1:T(8,128)} %param.19) | copy-start | bytes 4612
Sparse Core Ops, SparseCore 0:
  305.2 100.7 reduce-scatter.1
